TPU v7x, 512 devices: a whole 4x8x8 slice. The times are simulated.
512 devices in a mesh: seq: 128 (over y, z, core), sub: 4 (over x).
Axes of the slice: x: 4, y: 8, z: 8, core: 2. Of those that a mesh axis runs over, the one named last changes fastest.
Arguments:
- linear_query: bfloat16 [32768, 256], P(('seq', 'sub')), may hold values from -6 to 6
- linear_key: bfloat16 [32768, 256], P(('seq', 'sub')), may hold values from -6 to 6
- linear_value: bfloat16 [32768, 2048], P(('seq', 'sub')), may hold values from -6 to 6
- lin_gain: float32 [2048], replicated, may hold values from 0.1 to 1.9
- window_query: bfloat16 [32768, 2048], P(('seq', 'sub')), may hold values from -6 to 6
- window_key: bfloat16 [32768, 2048], P(('seq', 'sub')), may hold values from -6 to 6
- window_value: bfloat16 [32768, 2048], P(('seq', 'sub')), may hold values from -6 to 6
Outputs:
- linear_out: bfloat16 [32768, 2048], P(('seq', 'sub'))
- window_out: bfloat16 [32768, 2048], P(('seq', 'sub'))
All inputs are finite; a program needn't handle non-finite values.
Results may differ from a plain program's by a relative error of at most 0.007.
Values may be sent and summed in bfloat16 or wider, within the bound.
No kernel may reach another device: no remote copies, remote signals or barrier semaphores. Data moves between devices by JAX's collectives and lax.ppermute only.
A program may use at most 128 MiB of HBM per device.

v0:
```python
import math
import jax
import jax.numpy as jnp
import numpy as np
from jax import lax
from jax.sharding import Mesh
from jax.sharding import PartitionSpec as P

FDIM = 16
VDIM = 128
SDIM = 128
WINDOW = 512
CORES = 2
FEAT_PAD = 160
ALL = ("y", "z", "core", "sub")
GROUP = ("core", "sub")


def pair_tables(for_query):
    pairs = [(0, 0)] + [(0, a + 1) for a in range(FDIM)]
    pairs += [(a + 1, b + 1) for a in range(FDIM) for b in range(a, FDIM)]
    first = np.zeros((FDIM + 1, FEAT_PAD), np.float32)
    second = np.zeros((FDIM + 1, FEAT_PAD), np.float32)
    for f, (a, b) in enumerate(pairs):
        first[a, f] = 0.5 if for_query and a == b and (a > 0) else 1.0
        second[b, f] = 1.0
    return (first, second)


def passed_along(shard, axis, by):
    size = lax.axis_size(axis)
    pairs = [(i, i + by) for i in range(size) if 0 <= i + by < size]
    return lax.ppermute(shard, axis, pairs)


def sym_features(vectors, for_query):
    halved = vectors * 0.5
    ext = jnp.concatenate([jnp.ones(halved.shape[:-1] + (1,), jnp.float32), halved], axis=-1)
    first, second = pair_tables(for_query)
    pick = lambda table: jnp.einsum(
        "jhi,if->jhf", ext, jnp.asarray(table), precision=lax.Precision.HIGHEST
    )
    return pick(first) * pick(second)


def groups_before(total):
    z_count = lax.axis_size("z")
    heads, feats, width = total.shape
    dealt = total.reshape(heads, z_count, feats // z_count, width)
    held = lax.all_to_all(dealt, "z", split_axis=1, concat_axis=1, tiled=True)
    running = jnp.cumsum(held, axis=1)
    line_total = running[:, -1]
    along_y = lax.all_gather(line_total, "y")
    y_before = jnp.arange(along_y.shape[0]) < lax.axis_index("y")
    lines_before = jnp.sum(jnp.where(y_before[:, None, None, None], along_y, 0.0), axis=0)
    prefix = running - held + lines_before[:, None]
    back = lax.all_to_all(prefix, "z", split_axis=1, concat_axis=1, tiled=True)
    return back.reshape(heads, feats, width)


def linear_heads(linear_query, linear_key, linear_value, lin_gain):
    rows_dev = linear_query.shape[0]
    group_count = lax.axis_size(GROUP)
    lin_heads = linear_query.shape[1] // FDIM
    own_heads = lin_heads // group_count
    packed = jnp.concatenate(
        [
            linear_query.reshape(rows_dev, group_count, own_heads * FDIM),
            linear_key.reshape(rows_dev, group_count, own_heads * FDIM),
            linear_value.reshape(rows_dev, group_count, own_heads * VDIM),
        ],
        axis=-1,
    )
    got = lax.all_to_all(packed, GROUP, split_axis=1, concat_axis=0, tiled=True)
    rows = got.shape[0]
    got = got.reshape(rows, -1)
    query_bf = got[:, : own_heads * FDIM].reshape(rows, own_heads, FDIM)
    key_bf = got[:, own_heads * FDIM : 2 * own_heads * FDIM].reshape(rows, own_heads, FDIM)
    value_lin = got[:, 2 * own_heads * FDIM :].reshape(rows, own_heads, VDIM).astype(jnp.float32)
    query_lin = query_bf.astype(jnp.float32)
    key_lin = key_bf.astype(jnp.float32)
    total = jnp.einsum(
        "jhf,jhe->hfe", sym_features(key_lin, False), value_lin, precision=lax.Precision.HIGHEST
    )
    before = groups_before(total)
    from_state = jnp.einsum(
        "ihf,hfe->ihe", sym_features(query_lin, True), before, precision=lax.Precision.HIGHEST
    )
    dot_inner = (
        jnp.einsum("ihd,jhd->hij", query_bf, key_bf, preferred_element_type=jnp.float32) * 0.25
    )
    weight = 1.0 + dot_inner + 0.5 * dot_inner * dot_inner
    causal = (
        jnp.arange(rows, dtype=jnp.int32)[:, None] >= jnp.arange(rows, dtype=jnp.int32)[None, :]
    )
    weight = jnp.where(causal[None], weight, jnp.float32(0.0))
    local_sum = jnp.einsum("hij,jhe->ihe", weight, value_lin, precision=lax.Precision.HIGHEST)
    numerator = local_sum + from_state
    inv_rms = lax.rsqrt(jnp.mean(numerator * numerator, axis=-1, keepdims=True) + 1e-05)
    gain_rows = lax.dynamic_slice_in_dim(
        lin_gain.reshape(lin_heads, VDIM), lax.axis_index(GROUP) * own_heads, own_heads, 0
    )
    out = (numerator * inv_rms * gain_rows).astype(jnp.bfloat16)
    out = out.reshape(group_count, rows_dev, own_heads * VDIM)
    back = lax.all_to_all(out, GROUP, split_axis=0, concat_axis=2, tiled=True)
    return back.reshape(rows_dev, lin_heads * VDIM)


def shards(
    linear_query, linear_key, linear_value, lin_gain, window_query, window_key, window_value
):
    rows_dev = linear_query.shape[0]
    dev_count = lax.axis_size(ALL)
    group_count = lax.axis_size(GROUP)
    device_pos = lax.axis_index(ALL)
    base_row = device_pos * rows_dev
    reach_dev = WINDOW // rows_dev
    channels = window_key.shape[1]
    head_count = channels // SDIM
    lin_heads = linear_query.shape[1] // FDIM
    stacked = jnp.stack([window_key, window_value])
    earlier = [passed_along(stacked, ALL, reach_dev - t) for t in range(reach_dev)]
    earlier = jnp.concatenate(earlier, axis=1)
    key_rows = jnp.concatenate([earlier[0], window_key], axis=0).reshape(-1, head_count, SDIM)
    value_rows = jnp.concatenate([earlier[1], window_value], axis=0).reshape(-1, head_count, SDIM)
    query_heads = window_query.reshape(rows_dev, head_count, SDIM)
    scores = jnp.einsum(
        "ihd,jhd->hij", query_heads, key_rows, preferred_element_type=jnp.float32
    ) * (1.0 / math.sqrt(SDIM))
    query_pos = base_row + jnp.arange(rows_dev, dtype=jnp.int32)
    key_pos = (
        base_row - reach_dev * rows_dev + jnp.arange((reach_dev + 1) * rows_dev, dtype=jnp.int32)
    )
    allowed = (
        (key_pos[None, :] <= query_pos[:, None])
        & (key_pos[None, :] > query_pos[:, None] - WINDOW)
        & (key_pos[None, :] >= 0)
    )
    scores = jnp.where(allowed[None], scores, jnp.float32(-1e30))
    row_max = jnp.max(scores, axis=-1, keepdims=True)
    exp_scores = jnp.exp(scores - row_max)
    weights_bf = (exp_scores / jnp.sum(exp_scores, axis=-1, keepdims=True)).astype(jnp.bfloat16)
    mixed = jnp.einsum("hij,jhd->ihd", weights_bf, value_rows, preferred_element_type=jnp.float32)
    window_out = mixed.reshape(rows_dev, channels).astype(jnp.bfloat16)
    linear_out = linear_heads(linear_query, linear_key, linear_value, lin_gain)
    return (linear_out, window_out)


def solution(mesh):
    seq_count = mesh.shape["seq"]
    sub_count = mesh.shape["sub"]
    lines = seq_count // CORES
    z_count = math.isqrt(lines)
    split_mesh = Mesh(
        np.asarray(mesh.devices).reshape(lines // z_count, z_count, CORES, sub_count), ALL
    )
    rows = P(ALL, None)
    in_specs = (rows, rows, rows, P(), rows, rows, rows)
    out_specs = (rows, rows)
    return jax.shard_map(
        shards, mesh=split_mesh, in_specs=in_specs, out_specs=out_specs, check_vma=False
    )
```

profile of v0, /device:TPU:1, one launch (start us, length us, event | category | flops | bytes accessed | tf_op | source)
XLA Modules:
  0.0 187.4 jit_solution(14541325597579867296)
XLA Ops:
  2.7 4.8 %collective-permute-start = (bf16[2,64,2048]{2,1,0:T(8,128)(2,1)}, bf16[2,64,2048]{2,1,0:T(8,128)(2,1)S(1)}, u32[]{:S(2)}, u32[]{:S(2)}) collective-permute-start(bf16[2,64,2048]{2,1,0:T(8,128)(2,1)} %pad_maximum_fusion), channel_id=1, source_target_pairs={{0,8},{1,9},{2,10},{3,11},{4,12},{5,13},{6,14},{7,15},{8,16},{9,17... | collective-permute-start | bytes 1572872 | tf_op jit(solution)/shard_map/ppermute | solution.py:33
  7.5 7.0 %collective-permute-start.1 = (bf16[2,64,2048]{2,1,0:T(8,128)(2,1)}, bf16[2,64,2048]{2,1,0:T(8,128)(2,1)S(1)}, u32[]{:S(2)}, u32[]{:S(2)}) collective-permute-start(bf16[2,64,2048]{2,1,0:T(8,128)(2,1)} %pad_maximum_fusion), channel_id=1, source_target_pairs={{0,7},{1,8},{2,9},{3,10},{4,11},{5,12},{6,13},{7,14},{8,15},{9,16}... | collective-permute-start | bytes 1572872 | tf_op jit(solution)/shard_map/ppermute | solution.py:33
  14.6 4.5 %collective-permute-start.2 = (bf16[2,64,2048]{2,1,0:T(8,128)(2,1)}, bf16[2,64,2048]{2,1,0:T(8,128)(2,1)S(1)}, u32[]{:S(2)}, u32[]{:S(2)}) collective-permute-start(bf16[2,64,2048]{2,1,0:T(8,128)(2,1)} %pad_maximum_fusion), channel_id=1, source_target_pairs={{0,6},{1,7},{2,8},{3,9},{4,10},{5,11},{6,12},{7,13},{8,14},{9,15},... | collective-permute-start | bytes 1572872 | tf_op jit(solution)/shard_map/ppermute | solution.py:33
  19.1 2.5 %collective-permute-start.3 = (bf16[2,64,2048]{2,1,0:T(8,128)(2,1)}, bf16[2,64,2048]{2,1,0:T(8,128)(2,1)}, u32[]{:S(2)}, u32[]{:S(2)}) collective-permute-start(bf16[2,64,2048]{2,1,0:T(8,128)(2,1)} %pad_maximum_fusion), channel_id=1, source_target_pairs={{0,5},{1,6},{2,7},{3,8},{4,9},{5,10},{6,11},{7,12},{8,13},{9,14},{... | collective-permute-start | bytes 1572872 | tf_op jit(solution)/shard_map/ppermute | solution.py:33
  21.6 5.5 %collective-permute-start.4 = (bf16[2,64,2048]{2,1,0:T(8,128)(2,1)}, bf16[2,64,2048]{2,1,0:T(8,128)(2,1)}, u32[]{:S(2)}, u32[]{:S(2)}) collective-permute-start(bf16[2,64,2048]{2,1,0:T(8,128)(2,1)} %pad_maximum_fusion), channel_id=1, source_target_pairs={{0,4},{1,5},{2,6},{3,7},{4,8},{5,9},{6,10},{7,11},{8,12},{9,13},{1... | collective-permute-start | bytes 1572872 | tf_op jit(solution)/shard_map/ppermute | solution.py:33
  31.1 4.5 %all-to-all-start = ((bf16[64,8,320]{2,0,1:T(8,128)(2,1)}), bf16[64,8,320]{2,0,1:T(8,128)(2,1)S(1)}, u32[]{:S(2)}, u32[]{:S(2)}) async-start(bf16[64,8,320]{2,0,1:T(8,128)(2,1)} %pad_maximum_fusion.1), calls=%async_computation | async-start | bytes 786432 | tf_op jit(solution)/shard_map/all_to_all | solution.py:74
  38.1 5.5 %all-to-all-done = bf16[64,8,320]{2,0,1:T(8,128)(2,1)S(1)} async-done(((bf16[64,8,320]{2,0,1:T(8,128)(2,1)}), bf16[64,8,320]{2,0,1:T(8,128)(2,1)S(1)}, u32[]{:S(2)}, u32[]{:S(2)}) %all-to-all-start) | async-done | bytes 327712 | tf_op jit(solution)/shard_map/all_to_all | solution.py:74
  46.8 25.6 %all-to-all-start.1 = ((f32[2,8,20,128]{3,0,2,1:T(2,128)}), f32[2,8,20,128]{3,0,2,1:T(2,128)}, u32[]{:S(2)}, u32[]{:S(2)}) async-start(f32[2,8,20,128]{3,0,2,1:T(2,128)} %bitcast.12), calls=%async_computation.1 | async-start | bytes 327680 | tf_op jit(solution)/shard_map/all_to_all | solution.py:50
  77.6 5.4 %collective-permute-start.7 = (bf16[2,64,2048]{2,1,0:T(8,128)(2,1)}, bf16[2,64,2048]{2,1,0:T(8,128)(2,1)}, u32[]{:S(2)}, u32[]{:S(2)}) collective-permute-start(bf16[2,64,2048]{2,1,0:T(8,128)(2,1)} %pad_maximum_fusion), channel_id=1, source_target_pairs={{0,1},{1,2},{2,3},{3,4},{4,5},{5,6},{6,7},{7,8},{8,9},{9,10},{10,1... | collective-permute-start | bytes 1572872 | tf_op jit(solution)/shard_map/ppermute | solution.py:33
  84.6 2.6 %fusion.9 = f32[2,128,512]{2,1,0:T(8,128)} fusion(bf16[512,2,128]{0,2,1:T(8,128)(2,1)S(1)} %bitcast.98, f32[2,512,512]{2,1,0:T(8,128)S(1)} %fusion.75, pred[512,512]{1,0:T(8,128)(4,1)S(1)} %iota_compare_fusion), kind=kOutput, calls=%fused_computation.12 | convolution fusion | flops 808452096 | bytes 3145728 | tf_op jit(solution)/shard_map/hij,jhe->ihe/dot_general | solution.py:97
  92.0 2.4 %copy.105 = bf16[2,64,2048]{1,2,0:T(8,128)(2,1)} copy(bf16[2,64,2048]{2,1,0:T(8,128)(2,1)} %collective-permute-done.4) | data formatting | bytes 1048576 | tf_op jit(solution)/shard_map/ppermute | solution.py:33
  94.4 3.7 %collective-permute-done.5 = bf16[2,64,2048]{2,1,0:T(8,128)(2,1)} collective-permute-done((bf16[2,64,2048]{2,1,0:T(8,128)(2,1)}, bf16[2,64,2048]{2,1,0:T(8,128)(2,1)}, u32[]{:S(2)}, u32[]{:S(2)}) %collective-permute-start.5) | collective-permute-done | bytes 524320 | tf_op jit(solution)/shard_map/ppermute | solution.py:33
  98.1 2.4 %copy.106 = bf16[2,64,2048]{1,2,0:T(8,128)(2,1)} copy(bf16[2,64,2048]{2,1,0:T(8,128)(2,1)} %collective-permute-done.5) | data formatting | bytes 1048576 | tf_op jit(solution)/shard_map/ppermute | solution.py:33
  100.5 2.4 %copy.107 = bf16[2,64,2048]{1,2,0:T(8,128)(2,1)} copy(bf16[2,64,2048]{2,1,0:T(8,128)(2,1)} %collective-permute-done.6) | data formatting | bytes 1048576 | tf_op jit(solution)/shard_map/ppermute | solution.py:33
  103.0 2.4 %copy.108 = bf16[2,64,2048]{1,2,0:T(8,128)(2,1)} copy(bf16[2,64,2048]{2,1,0:T(8,128)(2,1)} %collective-permute-done.7) | data formatting | bytes 1048576 | tf_op jit(solution)/shard_map/ppermute | solution.py:33
  105.4 10.8 %concatenate.31 = bf16[2,512,2048]{1,2,0:T(8,128)(2,1)} concatenate(bf16[2,64,2048]{1,2,0:T(8,128)(2,1)S(1)} %copy.101, bf16[2,64,2048]{1,2,0:T(8,128)(2,1)S(1)} %copy.102, bf16[2,64,2048]{1,2,0:T(8,128)(2,1)S(1)} %copy.103, bf16[2,64,2048]{1,2,0:T(8,128)(2,1)} %copy.104, bf16[2,64,2048]{1,2,0:T(8,128)(2,1)} %copy.105, bf16[2,64,2048]{1,2,0:T(8,128)(2,1)} %copy.106, ...), dimensions={1} | concatenate | bytes 8388608 | tf_op jit(solution)/shard_map/concatenate | solution.py:123
  116.1 3.9 %fusion.67 = (bf16[1,512,2048]{1,2,0:T(8,128)(2,1)}, bf16[1,512,2048]{1,2,0:T(8,128)(2,1)S(1)}) fusion(bf16[2,512,2048]{1,2,0:T(8,128)(2,1)} %concatenate.31), kind=kLoop, calls=%fused_computation.77 | loop fusion | bytes 8388608 | tf_op jit(solution)/shard_map/slice | solution.py:124
  120.0 3.9 %copy.111 = bf16[512,16,128]{2,0,1:T(8,128)(2,1)} copy(bf16[512,16,128]{0,2,1:T(8,128)(2,1)} %bitcast.90) | data formatting | bytes 4194304 | tf_op jit(solution)/shard_map/concatenate | solution.py:124
  127.3 22.0 %all-gather = f32[16,1,20,128]{3,1,2,0:T(1,128)S(1)} all-gather(f32[2,1,20,128]{3,1,2,0:T(1,128)S(1)} %copy.96), channel_id=2, replica_groups=mesh['y'=8,'z'=8,'core'=2,'sub'=4] {'y'}, dimensions={0}, use_global_device_ids=true | all-gather | bytes 184320 | tf_op jit(solution)/shard_map/all_gather | solution.py:53
  151.1 6.7 %all-to-all-start.2 = ((f32[2,8,20,128]{3,0,2,1:T(2,128)}), f32[2,8,20,128]{3,0,2,1:T(2,128)S(1)}, u32[]{:S(2)}, u32[]{:S(2)}) async-start(f32[2,8,20,128]{3,0,2,1:T(2,128)} %bitcast.88), calls=%async_computation.2 | async-start | bytes 327680 | tf_op jit(solution)/shard_map/all_to_all | solution.py:57
  157.9 4.3 %fusion.69 = (f32[16,64]{1,0:T(8,128)S(1)}, f32[16,64,576]{2,1,0:T(8,128)}) fusion(pred[64,576]{1,0:T(8,128)(4,1)S(1)} %and_and_fusion, bf16[64,16,128]{2,0,1:T(8,128)(2,1)S(1)} %copy-done.7, bf16[512,16,128]{2,0,1:T(8,128)(2,1)} %copy.111, bf16[64,2048]{1,0:T(8,128)(2,1)S(1)} %copy-done), kind=kOutput, calls=%fused_computation.79 | convolution fusion | flops 158073408 | bytes 5021696 | tf_op jit(solution)/shard_map/sub | solution.py:141
  162.2 4.1 %all-to-all-done.2 = f32[2,8,20,128]{3,0,2,1:T(2,128)S(1)} async-done(((f32[2,8,20,128]{3,0,2,1:T(2,128)}), f32[2,8,20,128]{3,0,2,1:T(2,128)S(1)}, u32[]{:S(2)}, u32[]{:S(2)}) %all-to-all-start.2) | async-done | bytes 163872 | tf_op jit(solution)/shard_map/all_to_all | solution.py:57
  169.2 10.9 %all-to-all-start.3 = ((bf16[8,64,256]{2,1,0:T(8,128)(2,1)}), bf16[8,64,256]{2,1,0:T(8,128)(2,1)S(1)}, u32[]{:S(2)}, u32[]{:S(2)}) async-start(bf16[8,64,256]{2,1,0:T(8,128)(2,1)} %reshape.179), calls=%async_computation.3 | async-start | bytes 524288 | tf_op jit(solution)/shard_map/all_to_all | solution.py:105
  183.3 3.4 %all-to-all-done.3 = bf16[8,64,256]{2,1,0:T(8,128)(2,1)S(1)} async-done(((bf16[8,64,256]{2,1,0:T(8,128)(2,1)}), bf16[8,64,256]{2,1,0:T(8,128)(2,1)S(1)}, u32[]{:S(2)}, u32[]{:S(2)}) %all-to-all-start.3) | async-done | bytes 262176 | tf_op jit(solution)/shard_map/all_to_all | solution.py:105
  (81 shorter events, 35.1 us)
Async XLA Ops:
  0.6 157.3 %copy-start = (bf16[64,2048]{1,0:T(8,128)(2,1)S(1)}, bf16[64,2048]{1,0:T(8,128)(2,1)}, u32[]{:S(2)}) copy-start(bf16[64,2048]{1,0:T(8,128)(2,1)} %param.15) | copy-start | bytes 786436
  0.6 35.0 %copy-start.3 = (bf16[64,2048]{1,0:T(8,128)(2,1)S(1)}, bf16[64,2048]{1,0:T(8,128)(2,1)}, u32[]{:S(2)}) copy-start(bf16[64,2048]{1,0:T(8,128)(2,1)} %param.16) | copy-start | bytes 786436
  0.7 36.7 %copy-start.4 = (bf16[64,2048]{1,0:T(8,128)(2,1)S(1)}, bf16[64,2048]{1,0:T(8,128)(2,1)}, u32[]{:S(2)}) copy-start(bf16[64,2048]{1,0:T(8,128)(2,1)} %param.17) | copy-start | bytes 786436
  2.7 71.1 %collective-permute-start = (bf16[2,64,2048]{2,1,0:T(8,128)(2,1)}, bf16[2,64,2048]{2,1,0:T(8,128)(2,1)S(1)}, u32[]{:S(2)}, u32[]{:S(2)}) collective-permute-start(bf16[2,64,2048]{2,1,0:T(8,128)(2,1)} %pad_maximum_fusion), channel_id=1, source_target_pairs={{0,8},{1,9},{2,10},{3,11},{4,12},{5,13},{6,14},{7,15},{8,16},{9,17... | collective-permute-start | bytes 1572872 | tf_op jit(solution)/shard_map/ppermute | solution.py:33
  7.5 68.2 %collective-permute-start.1 = (bf16[2,64,2048]{2,1,0:T(8,128)(2,1)}, bf16[2,64,2048]{2,1,0:T(8,128)(2,1)S(1)}, u32[]{:S(2)}, u32[]{:S(2)}) collective-permute-start(bf16[2,64,2048]{2,1,0:T(8,128)(2,1)} %pad_maximum_fusion), channel_id=1, source_target_pairs={{0,7},{1,8},{2,9},{3,10},{4,11},{5,12},{6,13},{7,14},{8,15},{9,16}... | collective-permute-start | bytes 1572872 | tf_op jit(solution)/shard_map/ppermute | solution.py:33
  14.6 63.1 %collective-permute-start.2 = (bf16[2,64,2048]{2,1,0:T(8,128)(2,1)}, bf16[2,64,2048]{2,1,0:T(8,128)(2,1)S(1)}, u32[]{:S(2)}, u32[]{:S(2)}) collective-permute-start(bf16[2,64,2048]{2,1,0:T(8,128)(2,1)} %pad_maximum_fusion), channel_id=1, source_target_pairs={{0,6},{1,7},{2,8},{3,9},{4,10},{5,11},{6,12},{7,13},{8,14},{9,15},... | collective-permute-start | bytes 1572872 | tf_op jit(solution)/shard_map/ppermute | solution.py:33
  19.1 70.6 %collective-permute-start.3 = (bf16[2,64,2048]{2,1,0:T(8,128)(2,1)}, bf16[2,64,2048]{2,1,0:T(8,128)(2,1)}, u32[]{:S(2)}, u32[]{:S(2)}) collective-permute-start(bf16[2,64,2048]{2,1,0:T(8,128)(2,1)} %pad_maximum_fusion), channel_id=1, source_target_pairs={{0,5},{1,6},{2,7},{3,8},{4,9},{5,10},{6,11},{7,12},{8,13},{9,14},{... | collective-permute-start | bytes 1572872 | tf_op jit(solution)/shard_map/ppermute | solution.py:33
  21.6 70.5 %collective-permute-start.4 = (bf16[2,64,2048]{2,1,0:T(8,128)(2,1)}, bf16[2,64,2048]{2,1,0:T(8,128)(2,1)}, u32[]{:S(2)}, u32[]{:S(2)}) collective-permute-start(bf16[2,64,2048]{2,1,0:T(8,128)(2,1)} %pad_maximum_fusion), channel_id=1, source_target_pairs={{0,4},{1,5},{2,6},{3,7},{4,8},{5,9},{6,10},{7,11},{8,12},{9,13},{1... | collective-permute-start | bytes 1572872 | tf_op jit(solution)/shard_map/ppermute | solution.py:33
  30.1 14.0 %copy-start.10 = (f32[17,160,1]{1,0,2:T(8,128)S(1)}, f32[17,160,1]{1,0,2:T(8,128)}, u32[]{:S(2)}) copy-start(f32[17,160,1]{1,0,2:T(8,128)} %constant.80) | copy-start | bytes 32644
  31.1 13.7 %copy-start.8 = (f32[17,160,1]{1,0,2:T(8,128)S(1)}, f32[17,160,1]{1,0,2:T(8,128)}, u32[]{:S(2)}) copy-start(f32[17,160,1]{1,0,2:T(8,128)} %constant.81) | copy-start | bytes 32644
  31.1 12.5 %all-to-all-start = ((bf16[64,8,320]{2,0,1:T(8,128)(2,1)}), bf16[64,8,320]{2,0,1:T(8,128)(2,1)S(1)}, u32[]{:S(2)}, u32[]{:S(2)}) async-start(bf16[64,8,320]{2,0,1:T(8,128)(2,1)} %pad_maximum_fusion.1), calls=%async_computation | async-start | bytes 786432 | tf_op jit(solution)/shard_map/all_to_all | solution.py:74
  43.9 28.6 %copy-start.9 = (f32[17,160,1]{1,0,2:T(8,128)S(1)}, f32[17,160,1]{1,0,2:T(8,128)}, u32[]{:S(2)}) copy-start(f32[17,160,1]{1,0,2:T(8,128)} %constant.82) | copy-start | bytes 32644
  46.8 79.5 %all-to-all-start.1 = ((f32[2,8,20,128]{3,0,2,1:T(2,128)}), f32[2,8,20,128]{3,0,2,1:T(2,128)}, u32[]{:S(2)}, u32[]{:S(2)}) async-start(f32[2,8,20,128]{3,0,2,1:T(2,128)} %bitcast.12), calls=%async_computation.1 | async-start | bytes 327680 | tf_op jit(solution)/shard_map/all_to_all | solution.py:50
  73.8 24.4 %collective-permute-start.5 = (bf16[2,64,2048]{2,1,0:T(8,128)(2,1)}, bf16[2,64,2048]{2,1,0:T(8,128)(2,1)}, u32[]{:S(2)}, u32[]{:S(2)}) collective-permute-start(bf16[2,64,2048]{2,1,0:T(8,128)(2,1)} %pad_maximum_fusion), channel_id=1, source_target_pairs={{0,3},{1,4},{2,5},{3,6},{4,7},{5,8},{6,9},{7,10},{8,11},{9,12},{10... | collective-permute-start | bytes 1572872 | tf_op jit(solution)/shard_map/ppermute | solution.py:33
  75.7 24.8 %collective-permute-start.6 = (bf16[2,64,2048]{2,1,0:T(8,128)(2,1)}, bf16[2,64,2048]{2,1,0:T(8,128)(2,1)}, u32[]{:S(2)}, u32[]{:S(2)}) collective-permute-start(bf16[2,64,2048]{2,1,0:T(8,128)(2,1)} %pad_maximum_fusion), channel_id=1, source_target_pairs={{0,2},{1,3},{2,4},{3,5},{4,6},{5,7},{6,8},{7,9},{8,10},{9,11},{10,... | collective-permute-start | bytes 1572872 | tf_op jit(solution)/shard_map/ppermute | solution.py:33
  77.6 9.5 %copy-start.5 = (bf16[2,64,2048]{2,1,0:T(8,128)(2,1)}, bf16[2,64,2048]{2,1,0:T(8,128)(2,1)S(1)}, u32[]{:S(2)}) copy-start(bf16[2,64,2048]{2,1,0:T(8,128)(2,1)S(1)} %collective-permute-done.2) | copy-start | bytes 1572868
  77.6 25.3 %collective-permute-start.7 = (bf16[2,64,2048]{2,1,0:T(8,128)(2,1)}, bf16[2,64,2048]{2,1,0:T(8,128)(2,1)}, u32[]{:S(2)}, u32[]{:S(2)}) collective-permute-start(bf16[2,64,2048]{2,1,0:T(8,128)(2,1)} %pad_maximum_fusion), channel_id=1, source_target_pairs={{0,1},{1,2},{2,3},{3,4},{4,5},{5,6},{6,7},{7,8},{8,9},{9,10},{10,1... | collective-permute-start | bytes 1572872 | tf_op jit(solution)/shard_map/ppermute | solution.py:33
  123.9 33.9 %copy-start.7 = (bf16[64,16,128]{2,0,1:T(8,128)(2,1)S(1)}, bf16[64,16,128]{2,0,1:T(8,128)(2,1)}, u32[]{:S(2)}) copy-start(bf16[64,16,128]{2,0,1:T(8,128)(2,1)} %copy_bitcast_fusion.2) | copy-start | bytes 786436
  151.1 15.1 %all-to-all-start.2 = ((f32[2,8,20,128]{3,0,2,1:T(2,128)}), f32[2,8,20,128]{3,0,2,1:T(2,128)S(1)}, u32[]{:S(2)}, u32[]{:S(2)}) async-start(f32[2,8,20,128]{3,0,2,1:T(2,128)} %bitcast.88), calls=%async_computation.2 | async-start | bytes 327680 | tf_op jit(solution)/shard_map/all_to_all | solution.py:57
  157.9 8.4 %copy-start.1 = (f32[512,2,160]{0,2,1:T(8,128)S(1)}, f32[512,2,160]{0,2,1:T(8,128)}, u32[]{:S(2)}) copy-start(f32[512,2,160]{0,2,1:T(8,128)} %convolution_multiply_fusion) | copy-start | bytes 1966084
  162.2 18.0 %copy-start.2 = (bf16[512,16,128]{2,0,1:T(8,128)(2,1)S(1)}, bf16[512,16,128]{2,0,1:T(8,128)(2,1)}, u32[]{:S(2)}) copy-start(bf16[512,16,128]{2,0,1:T(8,128)(2,1)} %copy.109) | copy-start | bytes 6291460
  162.2 18.0 %copy-start.6 = (bf16[64,16,128]{2,0,1:T(8,128)(2,1)S(1)}, bf16[64,16,128]{2,0,1:T(8,128)(2,1)}, u32[]{:S(2)}) copy-start(bf16[64,16,128]{2,0,1:T(8,128)(2,1)} %copy_bitcast_fusion.1) | copy-start | bytes 786436
  169.2 17.5 %all-to-all-start.3 = ((bf16[8,64,256]{2,1,0:T(8,128)(2,1)}), bf16[8,64,256]{2,1,0:T(8,128)(2,1)S(1)}, u32[]{:S(2)}, u32[]{:S(2)}) async-start(bf16[8,64,256]{2,1,0:T(8,128)(2,1)} %reshape.179), calls=%async_computation.3 | async-start | bytes 524288 | tf_op jit(solution)/shard_map/all_to_all | solution.py:105
where the time goes:
time: 189 us; the launch traced here: 187 us
  starting transfers between devices  81.4 us (43%)
  local copies, waits for them, and re-layouts  44.6 us (24%)
  blocking collectives  22 us (12%)
  waiting for transfers between devices  16.7 us (9%)
  matrix products  15.7 us (8%)
  other arithmetic  6.05 us (3%)
    ppermute x8, starting transfers between devices, passed_along(): return lax.ppermute(shard, axis, pairs)  33.6 us
    all_to_all x1, starting transfers between devices, groups_before(): held = lax.all_to_all(dealt, 'z', split_axis=1, concat_axis=1, tiled=True)  25.6 us
    all_gather x1, blocking collectives, groups_before(): along_y = lax.all_gather(line_total, 'y')  22 us
    ppermute x8, local copies, waits for them, and re-layouts, passed_along(): return lax.ppermute(shard, axis, pairs)  14.5 us
    all_to_all x1, starting transfers between devices, linear_heads(): back = lax.all_to_all(out, GROUP, split_axis=0, concat_axis=2, tiled=True)  10.9 us
    concatenate x1, local copies, waits for them, and re-layouts, shards(): earlier = jnp.concatenate(earlier, axis=1)  10.8 us
    all_to_all x1, starting transfers between devices, groups_before(): back = lax.all_to_all(prefix, 'z', split_axis=1, concat_axis=1, tiled=True)  6.74 us
    all_to_all x1, waiting for transfers between devices, linear_heads(): got = lax.all_to_all(packed, GROUP, split_axis=1, concat_axis=0, tiled=True)  5.46 us
  transfers between devices with their start and end apart: 12, of which 4 were waited for; matrix products, arithmetic and copies ran while one was open for 31% of the time, Pallas kernels for 0%

commit v1 on v0

--- a/solution.py
+++ b/solution.py
@@ -54,7 +54,9 @@
     y_before = jnp.arange(along_y.shape[0]) < lax.axis_index("y")
     lines_before = jnp.sum(jnp.where(y_before[:, None, None, None], along_y, 0.0), axis=0)
     prefix = running - held + lines_before[:, None]
-    back = lax.all_to_all(prefix, "z", split_axis=1, concat_axis=1, tiled=True)
+    back = jnp.concatenate(
+        lax.all_to_all(jnp.stack(jnp.split(prefix, lax.axis_size("z"), axis=1)), "z", 0, 0), axis=1
+    )
     return back.reshape(heads, feats, width)
 
 

time: 189 us -> 194 us (1.026)
  local copies, waits for them, and re-layouts: 44.6 us -> 49.4 us
    unnamed x25 -> x32, local copies, waits for them, and re-layouts: 2.52 us -> 6.74 us
  transfers between devices with their start and end apart: 12 -> 12, of which waited for: 4 -> 4; matrix products, arithmetic and copies ran while one was open for 31% -> 30% of each run, Pallas kernels for 0% -> 0%
where the time goes in v1:
time: 194 us; the launch traced here: 192 us
  starting transfers between devices  81.4 us (42%)
  local copies, waits for them, and re-layouts  49.4 us (25%)
  blocking collectives  22 us (11%)
  waiting for transfers between devices  16.7 us (9%)
  matrix products  15.7 us (8%)
  other arithmetic  5.38 us (3%)
    ppermute x8, starting transfers between devices, passed_along(): return lax.ppermute(shard, axis, pairs)  33.6 us
    all_to_all x1, starting transfers between devices, groups_before(): held = lax.all_to_all(dealt, 'z', split_axis=1, concat_axis=1, tiled=True)  25.6 us
    all_gather x1, blocking collectives, groups_before(): along_y = lax.all_gather(line_total, 'y')  22 us
    ppermute x8, local copies, waits for them, and re-layouts, passed_along(): return lax.ppermute(shard, axis, pairs)  14.5 us
    all_to_all x1, starting transfers between devices, linear_heads(): back = lax.all_to_all(out, GROUP, split_axis=0, concat_axis=2, tiled=True)  10.9 us
    concatenate x1, local copies, waits for them, and re-layouts, shards(): earlier = jnp.concatenate(earlier, axis=1)  10.8 us
    all_to_all x1, starting transfers between devices, groups_before(): lax.all_to_all(jnp.stack(jnp.split(prefix, lax.axis_size('z'), axis=1)),...  6.74 us
    unnamed x32, local copies, waits for them, and re-layouts  6.74 us
  transfers between devices with their start and end apart: 12, of which 4 were waited for; matrix products, arithmetic and copies ran while one was open for 30% of the time, Pallas kernels for 0%

profile of v1, /device:TPU:1, one launch (start us, length us, event | category | flops | bytes accessed | tf_op | source)
XLA Modules:
  0.0 191.6 jit_solution(7137685744046331396)
XLA Ops:
  2.7 4.8 %collective-permute-start = (bf16[2,64,2048]{2,1,0:T(8,128)(2,1)}, bf16[2,64,2048]{2,1,0:T(8,128)(2,1)S(1)}, u32[]{:S(2)}, u32[]{:S(2)}) collective-permute-start(bf16[2,64,2048]{2,1,0:T(8,128)(2,1)} %pad_maximum_fusion), channel_id=1, source_target_pairs={{0,8},{1,9},{2,10},{3,11},{4,12},{5,13},{6,14},{7,15},{8,16},{9,17... | collective-permute-start | bytes 1572872 | tf_op jit(solution)/shard_map/ppermute | solution.py:33
  7.5 7.0 %collective-permute-start.1 = (bf16[2,64,2048]{2,1,0:T(8,128)(2,1)}, bf16[2,64,2048]{2,1,0:T(8,128)(2,1)S(1)}, u32[]{:S(2)}, u32[]{:S(2)}) collective-permute-start(bf16[2,64,2048]{2,1,0:T(8,128)(2,1)} %pad_maximum_fusion), channel_id=1, source_target_pairs={{0,7},{1,8},{2,9},{3,10},{4,11},{5,12},{6,13},{7,14},{8,15},{9,16}... | collective-permute-start | bytes 1572872 | tf_op jit(solution)/shard_map/ppermute | solution.py:33
  14.6 4.5 %collective-permute-start.2 = (bf16[2,64,2048]{2,1,0:T(8,128)(2,1)}, bf16[2,64,2048]{2,1,0:T(8,128)(2,1)S(1)}, u32[]{:S(2)}, u32[]{:S(2)}) collective-permute-start(bf16[2,64,2048]{2,1,0:T(8,128)(2,1)} %pad_maximum_fusion), channel_id=1, source_target_pairs={{0,6},{1,7},{2,8},{3,9},{4,10},{5,11},{6,12},{7,13},{8,14},{9,15},... | collective-permute-start | bytes 1572872 | tf_op jit(solution)/shard_map/ppermute | solution.py:33
  19.1 2.5 %collective-permute-start.3 = (bf16[2,64,2048]{2,1,0:T(8,128)(2,1)}, bf16[2,64,2048]{2,1,0:T(8,128)(2,1)}, u32[]{:S(2)}, u32[]{:S(2)}) collective-permute-start(bf16[2,64,2048]{2,1,0:T(8,128)(2,1)} %pad_maximum_fusion), channel_id=1, source_target_pairs={{0,5},{1,6},{2,7},{3,8},{4,9},{5,10},{6,11},{7,12},{8,13},{9,14},{... | collective-permute-start | bytes 1572872 | tf_op jit(solution)/shard_map/ppermute | solution.py:33
  21.6 5.5 %collective-permute-start.4 = (bf16[2,64,2048]{2,1,0:T(8,128)(2,1)}, bf16[2,64,2048]{2,1,0:T(8,128)(2,1)}, u32[]{:S(2)}, u32[]{:S(2)}) collective-permute-start(bf16[2,64,2048]{2,1,0:T(8,128)(2,1)} %pad_maximum_fusion), channel_id=1, source_target_pairs={{0,4},{1,5},{2,6},{3,7},{4,8},{5,9},{6,10},{7,11},{8,12},{9,13},{1... | collective-permute-start | bytes 1572872 | tf_op jit(solution)/shard_map/ppermute | solution.py:33
  31.1 4.5 %all-to-all-start = ((bf16[64,8,320]{2,0,1:T(8,128)(2,1)}), bf16[64,8,320]{2,0,1:T(8,128)(2,1)S(1)}, u32[]{:S(2)}, u32[]{:S(2)}) async-start(bf16[64,8,320]{2,0,1:T(8,128)(2,1)} %pad_maximum_fusion.1), calls=%async_computation | async-start | bytes 786432 | tf_op jit(solution)/shard_map/all_to_all | solution.py:76
  38.1 5.5 %all-to-all-done = bf16[64,8,320]{2,0,1:T(8,128)(2,1)S(1)} async-done(((bf16[64,8,320]{2,0,1:T(8,128)(2,1)}), bf16[64,8,320]{2,0,1:T(8,128)(2,1)S(1)}, u32[]{:S(2)}, u32[]{:S(2)}) %all-to-all-start) | async-done | bytes 327712 | tf_op jit(solution)/shard_map/all_to_all | solution.py:76
  46.8 25.6 %all-to-all-start.1 = ((f32[2,8,20,128]{3,0,2,1:T(2,128)}), f32[2,8,20,128]{3,0,2,1:T(2,128)}, u32[]{:S(2)}, u32[]{:S(2)}) async-start(f32[2,8,20,128]{3,0,2,1:T(2,128)} %bitcast.12), calls=%async_computation.1 | async-start | bytes 327680 | tf_op jit(solution)/shard_map/all_to_all | solution.py:50
  77.6 5.4 %collective-permute-start.7 = (bf16[2,64,2048]{2,1,0:T(8,128)(2,1)}, bf16[2,64,2048]{2,1,0:T(8,128)(2,1)}, u32[]{:S(2)}, u32[]{:S(2)}) collective-permute-start(bf16[2,64,2048]{2,1,0:T(8,128)(2,1)} %pad_maximum_fusion), channel_id=1, source_target_pairs={{0,1},{1,2},{2,3},{3,4},{4,5},{5,6},{6,7},{7,8},{8,9},{9,10},{10,1... | collective-permute-start | bytes 1572872 | tf_op jit(solution)/shard_map/ppermute | solution.py:33
  84.6 2.6 %fusion.9 = f32[2,128,512]{2,1,0:T(8,128)} fusion(bf16[512,2,128]{0,2,1:T(8,128)(2,1)S(1)} %bitcast.132, f32[2,512,512]{2,1,0:T(8,128)S(1)} %fusion.83, pred[512,512]{1,0:T(8,128)(4,1)S(1)} %iota_compare_fusion), kind=kOutput, calls=%fused_computation.12 | convolution fusion | flops 808452096 | bytes 3145728 | tf_op jit(solution)/shard_map/hij,jhe->ihe/dot_general | solution.py:99
  92.0 2.4 %copy.113 = bf16[2,64,2048]{1,2,0:T(8,128)(2,1)} copy(bf16[2,64,2048]{2,1,0:T(8,128)(2,1)} %collective-permute-done.4) | data formatting | bytes 1048576 | tf_op jit(solution)/shard_map/ppermute | solution.py:33
  94.4 3.7 %collective-permute-done.5 = bf16[2,64,2048]{2,1,0:T(8,128)(2,1)} collective-permute-done((bf16[2,64,2048]{2,1,0:T(8,128)(2,1)}, bf16[2,64,2048]{2,1,0:T(8,128)(2,1)}, u32[]{:S(2)}, u32[]{:S(2)}) %collective-permute-start.5) | collective-permute-done | bytes 524320 | tf_op jit(solution)/shard_map/ppermute | solution.py:33
  98.1 2.4 %copy.114 = bf16[2,64,2048]{1,2,0:T(8,128)(2,1)} copy(bf16[2,64,2048]{2,1,0:T(8,128)(2,1)} %collective-permute-done.5) | data formatting | bytes 1048576 | tf_op jit(solution)/shard_map/ppermute | solution.py:33
  100.5 2.4 %copy.115 = bf16[2,64,2048]{1,2,0:T(8,128)(2,1)} copy(bf16[2,64,2048]{2,1,0:T(8,128)(2,1)} %collective-permute-done.6) | data formatting | bytes 1048576 | tf_op jit(solution)/shard_map/ppermute | solution.py:33
  103.0 2.4 %copy.116 = bf16[2,64,2048]{1,2,0:T(8,128)(2,1)} copy(bf16[2,64,2048]{2,1,0:T(8,128)(2,1)} %collective-permute-done.7) | data formatting | bytes 1048576 | tf_op jit(solution)/shard_map/ppermute | solution.py:33
  105.4 10.8 %concatenate.31 = bf16[2,512,2048]{1,2,0:T(8,128)(2,1)} concatenate(bf16[2,64,2048]{1,2,0:T(8,128)(2,1)S(1)} %copy.109, bf16[2,64,2048]{1,2,0:T(8,128)(2,1)S(1)} %copy.110, bf16[2,64,2048]{1,2,0:T(8,128)(2,1)S(1)} %copy.111, bf16[2,64,2048]{1,2,0:T(8,128)(2,1)} %copy.112, bf16[2,64,2048]{1,2,0:T(8,128)(2,1)} %copy.113, bf16[2,64,2048]{1,2,0:T(8,128)(2,1)} %copy.114, ...), dimensions={1} | concatenate | bytes 8388608 | tf_op jit(solution)/shard_map/concatenate | solution.py:125
  116.1 3.9 %fusion.75 = (bf16[1,512,2048]{1,2,0:T(8,128)(2,1)}, bf16[1,512,2048]{1,2,0:T(8,128)(2,1)S(1)}) fusion(bf16[2,512,2048]{1,2,0:T(8,128)(2,1)} %concatenate.31), kind=kLoop, calls=%fused_computation.93 | loop fusion | bytes 8388608 | tf_op jit(solution)/shard_map/slice | solution.py:126
  120.0 3.9 %copy.119 = bf16[512,16,128]{2,0,1:T(8,128)(2,1)} copy(bf16[512,16,128]{0,2,1:T(8,128)(2,1)} %bitcast.124) | data formatting | bytes 4194304 | tf_op jit(solution)/shard_map/concatenate | solution.py:126
  127.3 22.0 %all-gather = f32[16,1,20,128]{3,1,2,0:T(1,128)S(1)} all-gather(f32[2,1,20,128]{3,1,2,0:T(1,128)S(1)} %copy.104), channel_id=2, replica_groups=mesh['y'=8,'z'=8,'core'=2,'sub'=4] {'y'}, dimensions={0}, use_global_device_ids=true | all-gather | bytes 184320 | tf_op jit(solution)/shard_map/all_gather | solution.py:53
  155.3 6.7 %all-to-all-start.2 = ((f32[8,2,1,20,128]{4,1,3,2,0:T(2,128)}), f32[8,2,1,20,128]{4,1,3,2,0:T(2,128)S(1)}, u32[]{:S(2)}, u32[]{:S(2)}) async-start(f32[8,2,1,20,128]{4,1,3,2,0:T(2,128)} %fusion.49), calls=%async_computation.2 | async-start | bytes 327680 | tf_op jit(solution)/shard_map/all_to_all | solution.py:58
  162.1 4.3 %fusion.77 = (f32[16,64]{1,0:T(8,128)S(1)}, f32[16,64,576]{2,1,0:T(8,128)}) fusion(pred[64,576]{1,0:T(8,128)(4,1)S(1)} %and_and_fusion, bf16[64,16,128]{2,0,1:T(8,128)(2,1)S(1)} %copy-done.7, bf16[512,16,128]{2,0,1:T(8,128)(2,1)} %copy.119, bf16[64,2048]{1,0:T(8,128)(2,1)S(1)} %copy-done), kind=kOutput, calls=%fused_computation.95 | convolution fusion | flops 158073408 | bytes 5021696 | tf_op jit(solution)/shard_map/sub | solution.py:143
  166.3 4.1 %all-to-all-done.2 = f32[8,2,1,20,128]{4,1,3,2,0:T(2,128)S(1)} async-done(((f32[8,2,1,20,128]{4,1,3,2,0:T(2,128)}), f32[8,2,1,20,128]{4,1,3,2,0:T(2,128)S(1)}, u32[]{:S(2)}, u32[]{:S(2)}) %all-to-all-start.2) | async-done | bytes 163872 | tf_op jit(solution)/shard_map/all_to_all | solution.py:58
  173.4 10.9 %all-to-all-start.3 = ((bf16[8,64,256]{2,1,0:T(8,128)(2,1)}), bf16[8,64,256]{2,1,0:T(8,128)(2,1)S(1)}, u32[]{:S(2)}, u32[]{:S(2)}) async-start(bf16[8,64,256]{2,1,0:T(8,128)(2,1)} %reshape.179), calls=%async_computation.3 | async-start | bytes 524288 | tf_op jit(solution)/shard_map/all_to_all | solution.py:107
  187.4 3.4 %all-to-all-done.3 = bf16[8,64,256]{2,1,0:T(8,128)(2,1)S(1)} async-done(((bf16[8,64,256]{2,1,0:T(8,128)(2,1)}), bf16[8,64,256]{2,1,0:T(8,128)(2,1)S(1)}, u32[]{:S(2)}, u32[]{:S(2)}) %all-to-all-start.3) | async-done | bytes 262176 | tf_op jit(solution)/shard_map/all_to_all | solution.py:107
  (89 shorter events, 39.2 us)
Async XLA Ops:
  0.6 161.4 %copy-start = (bf16[64,2048]{1,0:T(8,128)(2,1)S(1)}, bf16[64,2048]{1,0:T(8,128)(2,1)}, u32[]{:S(2)}) copy-start(bf16[64,2048]{1,0:T(8,128)(2,1)} %param.15) | copy-start | bytes 786436
  0.6 35.0 %copy-start.3 = (bf16[64,2048]{1,0:T(8,128)(2,1)S(1)}, bf16[64,2048]{1,0:T(8,128)(2,1)}, u32[]{:S(2)}) copy-start(bf16[64,2048]{1,0:T(8,128)(2,1)} %param.16) | copy-start | bytes 786436
  0.7 36.7 %copy-start.4 = (bf16[64,2048]{1,0:T(8,128)(2,1)S(1)}, bf16[64,2048]{1,0:T(8,128)(2,1)}, u32[]{:S(2)}) copy-start(bf16[64,2048]{1,0:T(8,128)(2,1)} %param.17) | copy-start | bytes 786436
  2.7 71.1 %collective-permute-start = (bf16[2,64,2048]{2,1,0:T(8,128)(2,1)}, bf16[2,64,2048]{2,1,0:T(8,128)(2,1)S(1)}, u32[]{:S(2)}, u32[]{:S(2)}) collective-permute-start(bf16[2,64,2048]{2,1,0:T(8,128)(2,1)} %pad_maximum_fusion), channel_id=1, source_target_pairs={{0,8},{1,9},{2,10},{3,11},{4,12},{5,13},{6,14},{7,15},{8,16},{9,17... | collective-permute-start | bytes 1572872 | tf_op jit(solution)/shard_map/ppermute | solution.py:33
  7.5 68.2 %collective-permute-start.1 = (bf16[2,64,2048]{2,1,0:T(8,128)(2,1)}, bf16[2,64,2048]{2,1,0:T(8,128)(2,1)S(1)}, u32[]{:S(2)}, u32[]{:S(2)}) collective-permute-start(bf16[2,64,2048]{2,1,0:T(8,128)(2,1)} %pad_maximum_fusion), channel_id=1, source_target_pairs={{0,7},{1,8},{2,9},{3,10},{4,11},{5,12},{6,13},{7,14},{8,15},{9,16}... | collective-permute-start | bytes 1572872 | tf_op jit(solution)/shard_map/ppermute | solution.py:33
  14.6 63.1 %collective-permute-start.2 = (bf16[2,64,2048]{2,1,0:T(8,128)(2,1)}, bf16[2,64,2048]{2,1,0:T(8,128)(2,1)S(1)}, u32[]{:S(2)}, u32[]{:S(2)}) collective-permute-start(bf16[2,64,2048]{2,1,0:T(8,128)(2,1)} %pad_maximum_fusion), channel_id=1, source_target_pairs={{0,6},{1,7},{2,8},{3,9},{4,10},{5,11},{6,12},{7,13},{8,14},{9,15},... | collective-permute-start | bytes 1572872 | tf_op jit(solution)/shard_map/ppermute | solution.py:33
  19.1 70.6 %collective-permute-start.3 = (bf16[2,64,2048]{2,1,0:T(8,128)(2,1)}, bf16[2,64,2048]{2,1,0:T(8,128)(2,1)}, u32[]{:S(2)}, u32[]{:S(2)}) collective-permute-start(bf16[2,64,2048]{2,1,0:T(8,128)(2,1)} %pad_maximum_fusion), channel_id=1, source_target_pairs={{0,5},{1,6},{2,7},{3,8},{4,9},{5,10},{6,11},{7,12},{8,13},{9,14},{... | collective-permute-start | bytes 1572872 | tf_op jit(solution)/shard_map/ppermute | solution.py:33
  21.6 70.5 %collective-permute-start.4 = (bf16[2,64,2048]{2,1,0:T(8,128)(2,1)}, bf16[2,64,2048]{2,1,0:T(8,128)(2,1)}, u32[]{:S(2)}, u32[]{:S(2)}) collective-permute-start(bf16[2,64,2048]{2,1,0:T(8,128)(2,1)} %pad_maximum_fusion), channel_id=1, source_target_pairs={{0,4},{1,5},{2,6},{3,7},{4,8},{5,9},{6,10},{7,11},{8,12},{9,13},{1... | collective-permute-start | bytes 1572872 | tf_op jit(solution)/shard_map/ppermute | solution.py:33
  30.1 14.0 %copy-start.10 = (f32[17,160,1]{1,0,2:T(8,128)S(1)}, f32[17,160,1]{1,0,2:T(8,128)}, u32[]{:S(2)}) copy-start(f32[17,160,1]{1,0,2:T(8,128)} %constant.80) | copy-start | bytes 32644
  31.1 13.7 %copy-start.8 = (f32[17,160,1]{1,0,2:T(8,128)S(1)}, f32[17,160,1]{1,0,2:T(8,128)}, u32[]{:S(2)}) copy-start(f32[17,160,1]{1,0,2:T(8,128)} %constant.81) | copy-start | bytes 32644
  31.1 12.5 %all-to-all-start = ((bf16[64,8,320]{2,0,1:T(8,128)(2,1)}), bf16[64,8,320]{2,0,1:T(8,128)(2,1)S(1)}, u32[]{:S(2)}, u32[]{:S(2)}) async-start(bf16[64,8,320]{2,0,1:T(8,128)(2,1)} %pad_maximum_fusion.1), calls=%async_computation | async-start | bytes 786432 | tf_op jit(solution)/shard_map/all_to_all | solution.py:76
  43.9 28.6 %copy-start.9 = (f32[17,160,1]{1,0,2:T(8,128)S(1)}, f32[17,160,1]{1,0,2:T(8,128)}, u32[]{:S(2)}) copy-start(f32[17,160,1]{1,0,2:T(8,128)} %constant.82) | copy-start | bytes 32644
  46.8 79.5 %all-to-all-start.1 = ((f32[2,8,20,128]{3,0,2,1:T(2,128)}), f32[2,8,20,128]{3,0,2,1:T(2,128)}, u32[]{:S(2)}, u32[]{:S(2)}) async-start(f32[2,8,20,128]{3,0,2,1:T(2,128)} %bitcast.12), calls=%async_computation.1 | async-start | bytes 327680 | tf_op jit(solution)/shard_map/all_to_all | solution.py:50
  73.8 24.4 %collective-permute-start.5 = (bf16[2,64,2048]{2,1,0:T(8,128)(2,1)}, bf16[2,64,2048]{2,1,0:T(8,128)(2,1)}, u32[]{:S(2)}, u32[]{:S(2)}) collective-permute-start(bf16[2,64,2048]{2,1,0:T(8,128)(2,1)} %pad_maximum_fusion), channel_id=1, source_target_pairs={{0,3},{1,4},{2,5},{3,6},{4,7},{5,8},{6,9},{7,10},{8,11},{9,12},{10... | collective-permute-start | bytes 1572872 | tf_op jit(solution)/shard_map/ppermute | solution.py:33
  75.7 24.8 %collective-permute-start.6 = (bf16[2,64,2048]{2,1,0:T(8,128)(2,1)}, bf16[2,64,2048]{2,1,0:T(8,128)(2,1)}, u32[]{:S(2)}, u32[]{:S(2)}) collective-permute-start(bf16[2,64,2048]{2,1,0:T(8,128)(2,1)} %pad_maximum_fusion), channel_id=1, source_target_pairs={{0,2},{1,3},{2,4},{3,5},{4,6},{5,7},{6,8},{7,9},{8,10},{9,11},{10,... | collective-permute-start | bytes 1572872 | tf_op jit(solution)/shard_map/ppermute | solution.py:33
  77.6 9.5 %copy-start.5 = (bf16[2,64,2048]{2,1,0:T(8,128)(2,1)}, bf16[2,64,2048]{2,1,0:T(8,128)(2,1)S(1)}, u32[]{:S(2)}) copy-start(bf16[2,64,2048]{2,1,0:T(8,128)(2,1)S(1)} %collective-permute-done.2) | copy-start | bytes 1572868
  77.6 25.3 %collective-permute-start.7 = (bf16[2,64,2048]{2,1,0:T(8,128)(2,1)}, bf16[2,64,2048]{2,1,0:T(8,128)(2,1)}, u32[]{:S(2)}, u32[]{:S(2)}) collective-permute-start(bf16[2,64,2048]{2,1,0:T(8,128)(2,1)} %pad_maximum_fusion), channel_id=1, source_target_pairs={{0,1},{1,2},{2,3},{3,4},{4,5},{5,6},{6,7},{7,8},{8,9},{9,10},{10,1... | collective-permute-start | bytes 1572872 | tf_op jit(solution)/shard_map/ppermute | solution.py:33
  123.9 38.1 %copy-start.7 = (bf16[64,16,128]{2,0,1:T(8,128)(2,1)S(1)}, bf16[64,16,128]{2,0,1:T(8,128)(2,1)}, u32[]{:S(2)}) copy-start(bf16[64,16,128]{2,0,1:T(8,128)(2,1)} %copy_bitcast_fusion.2) | copy-start | bytes 786436
  155.3 15.1 %all-to-all-start.2 = ((f32[8,2,1,20,128]{4,1,3,2,0:T(2,128)}), f32[8,2,1,20,128]{4,1,3,2,0:T(2,128)S(1)}, u32[]{:S(2)}, u32[]{:S(2)}) async-start(f32[8,2,1,20,128]{4,1,3,2,0:T(2,128)} %fusion.49), calls=%async_computation.2 | async-start | bytes 327680 | tf_op jit(solution)/shard_map/all_to_all | solution.py:58
  162.1 8.4 %copy-start.1 = (f32[512,2,160]{0,2,1:T(8,128)S(1)}, f32[512,2,160]{0,2,1:T(8,128)}, u32[]{:S(2)}) copy-start(f32[512,2,160]{0,2,1:T(8,128)} %convolution_multiply_fusion) | copy-start | bytes 1966084
  166.3 18.0 %copy-start.2 = (bf16[512,16,128]{2,0,1:T(8,128)(2,1)S(1)}, bf16[512,16,128]{2,0,1:T(8,128)(2,1)}, u32[]{:S(2)}) copy-start(bf16[512,16,128]{2,0,1:T(8,128)(2,1)} %copy.117) | copy-start | bytes 6291460
  166.3 18.0 %copy-start.6 = (bf16[64,16,128]{2,0,1:T(8,128)(2,1)S(1)}, bf16[64,16,128]{2,0,1:T(8,128)(2,1)}, u32[]{:S(2)}) copy-start(bf16[64,16,128]{2,0,1:T(8,128)(2,1)} %copy_bitcast_fusion.1) | copy-start | bytes 786436
  173.4 17.5 %all-to-all-start.3 = ((bf16[8,64,256]{2,1,0:T(8,128)(2,1)}), bf16[8,64,256]{2,1,0:T(8,128)(2,1)S(1)}, u32[]{:S(2)}, u32[]{:S(2)}) async-start(bf16[8,64,256]{2,1,0:T(8,128)(2,1)} %reshape.179), calls=%async_computation.3 | async-start | bytes 524288 | tf_op jit(solution)/shard_map/all_to_all | solution.py:107
